TPU v7x, 32 devices: a whole 2x2x4 slice. The times are simulated.
32 devices in a mesh: req: 2 (over x), seq: 16 (over z, y, core).
Axes of the slice: x: 2, y: 2, z: 4, core: 2. Of those that a mesh axis runs over, the one named last changes fastest.
Arguments:
- states: bfloat16 [4, 4, 4544], P(None, 'req', 'seq'), may hold values from -6 to 6
- kv_cache: bfloat16 [4, 8192, 128], P('req', 'seq'), may hold values from -48 to 48, as said below
- lengths: int32 [4], replicated, may hold values from 1 to 8188, as said below
- placement: int32 [4], replicated, may hold values from 0 to 3, each once
- norm_gain: bfloat16 [4544], replicated, may hold values from 0.25 to 1.75
- norm_bias: bfloat16 [4544], replicated, may hold values from -1.5 to 1.5
- w_query: bfloat16 [4544, 4544], P('req', 'seq'), may hold values from -0.09375 to 0.09375
- w_keyval: bfloat16 [4544, 128], P('req'), may hold values from -0.09375 to 0.09375
- w_out: bfloat16 [4544, 4544], P('seq', 'req'), may hold values from -0.09375 to 0.09375
- w_up: bfloat16 [4544, 18176], P('req', 'seq'), may hold values from -0.09375 to 0.09375
- w_down: bfloat16 [18176, 4544], P('seq', 'req'), may hold values from -0.046875 to 0.046875
Outputs:
- new_states: bfloat16 [4, 4, 4544], P(None, 'req', 'seq')
- new_cache: bfloat16 [4, 8192, 128], P('req', 'seq')
Inputs may be any that keep to these rules, and one draw needn't show every extreme that they name: Request r's cache holds its first lengths[r] positions; some request has exactly 8188. `kv_cache`: row i is the cache of request placement[i]; positions at or beyond that request's length hold arbitrary values. `placement`: each request is served by exactly one slot.
All inputs are finite; a program needn't handle non-finite values.
Results may differ from a plain program's by a relative error of at most 0.012.
The roundings to bfloat16 on the way count: a program that leaves them out, or rounds other values in their place, can miss the bound.
Values may be sent and summed in bfloat16 or wider, within the bound.
No kernel may reach another device: no remote copies, remote signals or barrier semaphores. Data moves between devices by JAX's collectives and lax.ppermute only.
A program may use at most 192 MiB of HBM per device.

v0:
```python
import jax
import jax.numpy as jnp
from jax import lax
from jax.sharding import PartitionSpec as P

EPSILON = 1e-05
NEGATIVE = -1e30
ALL = ("req", "seq")


def layer_norm(row_block, norm_gain, norm_bias):
    values = row_block.astype(jnp.float32)
    average = jnp.mean(values, axis=-1, keepdims=True)
    centered = values - average
    spread = jnp.mean(centered * centered, axis=-1, keepdims=True)
    scaled = centered * lax.rsqrt(spread + EPSILON)
    return (scaled * norm_gain.astype(jnp.float32) + norm_bias.astype(jnp.float32)).astype(
        jnp.bfloat16
    )


def rotate(vectors, positions):
    head_width = vectors.shape[-1]
    half_width = head_width // 2
    frequency = 10000.0 ** (-(jnp.arange(half_width, dtype=jnp.float32) * 2.0) / head_width)
    angles = positions.astype(jnp.float32)[:, None] * frequency[None, :]
    cosine = jnp.concatenate([jnp.cos(angles), jnp.cos(angles)], axis=-1)[:, None, :]
    sine_wave = jnp.concatenate([jnp.sin(angles), jnp.sin(angles)], axis=-1)[:, None, :]
    turned = jnp.concatenate([-vectors[..., half_width:], vectors[..., :half_width]], axis=-1)
    return vectors * cosine + turned * sine_wave


def shards(
    states,
    kv_cache,
    lengths,
    placement,
    norm_gain,
    norm_bias,
    w_query,
    w_keyval,
    w_out,
    w_up,
    w_down,
):
    steps = states.shape[0]
    group_rows = kv_cache.shape[0]
    seg_length = kv_cache.shape[1]
    head_width = kv_cache.shape[2] // 2
    model_width = norm_gain.shape[0]
    head_count = model_width // head_width
    slice_width = states.shape[2]
    part_width = w_query.shape[0]
    total = placement.shape[0]
    req_size = total // group_rows
    seq_size = model_width // slice_width
    rows = steps * total
    group_index = lax.axis_index("req")
    shard_index = lax.axis_index("seq")
    own_requests = lax.dynamic_slice_in_dim(placement, group_index * group_rows, group_rows, 0)
    slot_lengths = jnp.take(lengths, own_requests)
    step_offsets = jnp.arange(steps, dtype=jnp.int32)
    positions = slot_lengths[None, :] + step_offsets[:, None]
    every = lax.all_gather(states, ALL, axis=0, tiled=False)
    every = every.reshape(req_size, seq_size, steps, group_rows, slice_width)
    every = every.transpose(2, 0, 3, 1, 4).reshape(steps, total, model_width)
    current_all = jnp.take(every, placement, axis=1)
    normed = layer_norm(current_all.reshape(rows, model_width), norm_gain, norm_bias)
    normed_part = lax.dynamic_slice_in_dim(normed, group_index * part_width, part_width, 1)
    part_query = jnp.dot(normed_part, w_query, preferred_element_type=jnp.float32)
    part_keyval = jnp.dot(normed_part, w_keyval, preferred_element_type=jnp.float32)
    part_up = jnp.dot(normed_part, w_up, preferred_element_type=jnp.float32)
    first = lax.psum(jnp.concatenate([part_query, part_keyval, part_up], axis=1), "req")
    query_raw = first[:, :slice_width].astype(jnp.bfloat16).reshape(steps, total, slice_width)
    keyval = first[:, slice_width : slice_width + 2 * head_width].reshape(
        steps, total, 2 * head_width
    )
    up_part = first[:, slice_width + 2 * head_width :]
    own_query = lax.dynamic_slice_in_dim(query_raw, group_index * group_rows, group_rows, 1)
    query_all = lax.all_gather(own_query, "seq", axis=2, tiled=True)
    flat_positions = positions.reshape(-1)
    query_rows = rotate(
        query_all.astype(jnp.float32).reshape(steps * group_rows, head_count, head_width),
        flat_positions,
    ).astype(jnp.bfloat16)
    own_keyval = lax.dynamic_slice_in_dim(keyval, group_index * group_rows, group_rows, 1)
    own_keyval = own_keyval.reshape(steps * group_rows, 2 * head_width)
    new_key = rotate(own_keyval[:, None, :head_width], flat_positions)[:, 0, :]
    new_entry = jnp.concatenate([new_key, own_keyval[:, head_width:]], axis=-1).astype(jnp.bfloat16)
    new_entry = new_entry.reshape(steps, group_rows, 2 * head_width)
    local_slots = jnp.arange(seg_length, dtype=jnp.int32)
    global_positions = shard_index * seg_length + local_slots
    cache_now = kv_cache
    for step_index in range(steps):
        write_mask = global_positions[None, :] == positions[step_index][:, None]
        cache_now = jnp.where(write_mask[:, :, None], new_entry[step_index][:, None, :], cache_now)
    key_rows = cache_now[:, :, :head_width]
    value_rows = cache_now[:, :, head_width:]
    query_heads = (
        query_rows.reshape(steps, group_rows, head_count, head_width)
        .transpose(1, 0, 2, 3)
        .reshape(group_rows, steps * head_count, head_width)
    )
    scores = jnp.einsum(
        "gqd,gsd->gqs", query_heads, key_rows, preferred_element_type=jnp.float32
    ) * head_width ** (-0.5)
    valid = global_positions[None, None, :] <= positions.T[:, :, None]
    valid = jnp.broadcast_to(
        valid[:, :, None, :], (group_rows, steps, head_count, seg_length)
    ).reshape(group_rows, steps * head_count, seg_length)
    local_peak = jnp.max(jnp.where(valid, scores, NEGATIVE), axis=-1)
    weights = jnp.where(valid, jnp.exp(scores - local_peak[:, :, None]), 0.0)
    local_total = jnp.sum(weights, axis=-1)
    local_weighted = jnp.einsum(
        "gqs,gsd->gqd", weights, value_rows, preferred_element_type=jnp.float32
    )
    peak_buffer = jnp.full((total, steps * head_count), NEGATIVE, jnp.float32)
    peak_buffer = lax.dynamic_update_slice_in_dim(
        peak_buffer, local_peak, group_index * group_rows, 0
    )
    peak = lax.pmax(peak_buffer, ALL)
    own_peak = lax.dynamic_slice_in_dim(peak, group_index * group_rows, group_rows, 0)
    scale = jnp.exp(local_peak - own_peak)
    packed = jnp.concatenate(
        [local_weighted * scale[:, :, None], (local_total * scale)[:, :, None]], axis=-1
    )
    packed_buffer = jnp.zeros((total, steps * head_count, head_width + 1), jnp.float32)
    packed_buffer = lax.dynamic_update_slice_in_dim(
        packed_buffer, packed, group_index * group_rows, 0
    )
    summed = lax.psum(packed_buffer, ALL)
    mixed = summed[:, :, :head_width] / summed[:, :, head_width:]
    mixed = (
        mixed.reshape(total, steps, model_width)
        .transpose(1, 0, 2)
        .reshape(rows, model_width)
        .astype(jnp.bfloat16)
    )
    mixed_part = lax.dynamic_slice_in_dim(mixed, shard_index * slice_width, slice_width, 1)
    hidden = jax.nn.gelu(up_part, approximate=False).astype(jnp.bfloat16)
    partial_sum = jnp.dot(mixed_part, w_out, preferred_element_type=jnp.float32) + jnp.dot(
        hidden, w_down, preferred_element_type=jnp.float32
    )
    out_buffer = jnp.zeros((rows, model_width), jnp.float32)
    out_buffer = lax.dynamic_update_slice_in_dim(
        out_buffer, partial_sum, group_index * part_width, 1
    )
    branch = lax.psum(out_buffer, ALL).reshape(steps, total, model_width)
    inverse = jnp.zeros((total,), jnp.int32).at[placement].set(jnp.arange(total, dtype=jnp.int32))
    own_inverse = lax.dynamic_slice_in_dim(inverse, group_index * group_rows, group_rows, 0)
    own_branch = jnp.take(branch, own_inverse, axis=1)
    own_branch = lax.dynamic_slice_in_dim(own_branch, shard_index * slice_width, slice_width, 2)
    new_states = (states.astype(jnp.float32) + own_branch).astype(jnp.bfloat16)
    return (new_states, cache_now)


def solution(mesh):
    in_specs = (
        P(None, "req", "seq"),
        P("req", "seq", None),
        P(),
        P(),
        P(),
        P(),
        P("req", "seq"),
        P("req", None),
        P("seq", "req"),
        P("req", "seq"),
        P("seq", "req"),
    )
    out_specs = (P(None, "req", "seq"), P("req", "seq", None))
    return jax.shard_map(shards, mesh=mesh, in_specs=in_specs, out_specs=out_specs, check_vma=False)
```

profile of v0, /device:TPU:8, one launch (start us, length us, event | category | flops | bytes accessed | tf_op | source)
XLA Modules:
  0.0 437.4 jit_solution(13402356280962080718)
XLA Ops:
  7.2 0.8 compare_select_fusion.2
  8.0 0.7 compare_and_fusion
  8.6 0.8 dynamic-slice.1
  9.4 0.8 dynamic-slice.2
  10.2 38.8 %all-gather = bf16[128,2,284]{2,1,0:T(2,128)(2,1)S(1)} all-gather(bf16[4,2,284]{2,1,0:T(2,128)(2,1)} %param.11), channel_id=2, replica_groups=mesh['req'=2,'seq'=16] {'req','seq'}, dimensions={0}, use_global_device_ids=true | all-gather | bytes 149952 | tf_op jit(solution)/shard_map/all_gather | solution.py:64
  49.0 0.3 reshape.348
  49.4 0.7 gather_fusion.1
  50.1 0.3 convert_reduce_fusion
  50.3 0.1 copy.70
  50.4 0.3 fusion.5
  50.7 0.1 copy.71
  50.8 0.1 rsqrt.12
  50.9 0.1 div.25
  51.1 0.1 broadcast_in_dim.144
  51.2 0.1 broadcast_select_fusion.1
  51.3 3.5 fusion.96
  54.8 0.3 fusion.94
  55.1 0.4 fusion.95
  55.5 0.8 concatenate.40
  56.5 0.6 gather_fusion
  57.4 0.1 multiply_cosine_fusion.1
  57.5 0.1 multiply_sine_fusion
  57.7 0.1 copy.81
  57.9 0.1 broadcast_in_dim.142
  58.0 0.2 reshape.346
  58.2 0.1 broadcast_compare_fusion.4
  58.3 19.3 %all-reduce.4.cloned.1.call-done = f32[16,1548]{1,0:T(8,128)} async-done(((f32[16,1548]{1,0:T(8,128)}), f32[16,1548]{1,0:T(8,128)}) %all-reduce.4.cloned.1.call-update) | async-done | bytes 99088 | tf_op jit(solution)/shard_map/psum | solution.py:73
  77.6 0.8 slice.99
  78.4 0.7 slice.124
  79.2 0.2 copy.88
  79.4 32.2 %all_gather.11 = bf16[4,2,4544]{0,1,2:T(2,128)(2,1)} all-gather(bf16[4,2,284]{0,1,2:T(2,128)(2,1)S(1)} %copy.88), channel_id=1, replica_groups=mesh['req'=2,'seq'=16] {'seq'}, dimensions={2}, use_global_device_ids=true | all-gather | bytes 77248 | tf_op jit(solution)/shard_map/all_gather | solution.py:80
  111.6 5.2 %copy.73 = bf16[4,2,4544]{2,0,1:T(4,128)(2,1)S(1)} copy(bf16[4,2,4544]{0,1,2:T(2,128)(2,1)} %all_gather.11) | data formatting | bytes 145408 | tf_op jit(solution)/shard_map/all_gather | solution.py:80
  116.8 0.2 reshape.351
  117.1 0.2 reshape.350
  117.6 0.1 fusion.98
  117.7 0.1 copy.89
  117.9 0.2 copy.78
  118.1 0.2 fusion.8
  118.2 0.2 copy.80
  118.4 0.1 reshape.352
  118.5 0.2 select_select_fusion
  118.8 0.5 select_reduce_fusion
  119.3 41.3 %pmax.7 = f32[4,284]{1,0:T(4,128)S(1)} all-reduce(f32[4,284]{1,0:T(4,128)S(1)} %constant_dynamic-update-slice_fusion.1), channel_id=1, replica_groups=mesh['req'=2,'seq'=16] {'req','seq'}, use_global_device_ids=true, to_apply=%region_5.6 | all-reduce | flops 1136 | bytes 9088 | tf_op jit(solution)/shard_map/pmax | solution.py:121
  160.6 0.4 fusion
  161.0 0.4 convolution_multiply_fusion.1
  161.5 0.2 copy.82
  161.7 0.8 copy-done.2
  162.6 0.6 scatter_custom_fusion
  163.2 129.3 %all-reduce.6.cloned.1.call-done = f32[4,284,65]{2,1,0:T(8,128)} async-done(((f32[4,284,65]{2,1,0:T(8,128)}), f32[4,284,65]{2,1,0:T(8,128)}) %all-reduce.6.cloned.1.call-update) | async-done | bytes 295376 | tf_op jit(solution)/shard_map/psum | solution.py:131
  292.5 1.5 slice_reduce_fusion
  294.0 1.3 fusion.1
  295.3 0.2 convert_element_type.69
  295.6 0.4 fusion.55
  296.0 0.2 copy-done.6
  296.2 3.4 convolution_add_fusion
  299.7 1.3 dynamic_update_slice.11
  301.0 0.1 reshape.355
  301.1 0.8 copy.84
  301.9 0.1 compare_and_fusion.1
  302.0 0.8 copy.86
  302.9 125.7 %all-reduce.8.cloned.1.call-done = f32[4,4,4544]{2,0,1:T(4,128)} async-done(((f32[4,4,4544]{2,0,1:T(4,128)}), f32[4,4,4544]{2,0,1:T(4,128)}) %all-reduce.8.cloned.1.call-update) | async-done | bytes 290832 | tf_op jit(solution)/shard_map/psum | solution.py:148
  428.5 1.6 gather_fusion.2
  430.1 0.1 fusion.54
  430.2 0.6 copy.85
  (65 shorter events, 1.6 us)
Async XLA Ops:
  7.2 288.4 %copy-start = (bf16[284,2272]{1,0:T(8,128)(2,1)S(1)}, bf16[284,2272]{1,0:T(8,128)(2,1)}, u32[]{:S(2)}) copy-start(bf16[284,2272]{1,0:T(8,128)(2,1)} %param.19) | copy-start | bytes 3871492
  7.2 70.4 %all-reduce.4.cloned.1.call-start = ((), (), s32[]{:S(2)}) async-start(), calls=%async_computation | async-start | bytes 212992 | tf_op jit(solution)/shard_map/psum | solution.py:73
  51.3 3.5 copy-start.4
  51.3 3.8 copy-start.3
  54.8 1.6 copy-start.8
  54.8 1.7 copy-start.1
  55.1 2.6 copy-start.5
  56.3 236.2 %all-reduce.6.cloned.1.call-start = ((), (), s32[]{:S(2)}) async-start(), calls=%async_computation.1 | async-start | bytes 1179648 | tf_op jit(solution)/shard_map/psum | solution.py:131
  161.7 0.8 copy-start.2
  162.6 266.0 %all-reduce.8.cloned.1.call-start = ((), (), s32[]{:S(2)}) async-start(), calls=%async_computation.2 | async-start | bytes 589824 | tf_op jit(solution)/shard_map/psum | solution.py:148
  295.3 0.9 copy-start.6
  301.0 129.2 %copy-start.7 = (bf16[4,2,284]{2,1,0:T(2,128)(2,1)S(1)}, bf16[4,2,284]{2,1,0:T(2,128)(2,1)}, u32[]{:S(2)}) copy-start(bf16[4,2,284]{2,1,0:T(2,128)(2,1)} %param.11) | copy-start | bytes 13636
Sparse Core Ops, SparseCore 0:
  56.4 21.1 all-reduce.3
  162.7 129.7 all-reduce.5
  302.1 126.4 all-reduce.7
where the time goes:
time: 438 us; the launch traced here: 437 us
  waiting for transfers between devices  274 us (63%)
  blocking collectives  112 us (26%)
  local copies, waits for them, and re-layouts  22.3 us (5%)
  between operations  14.2 us (3%)
  matrix products  8.89 us (2%)
  other arithmetic  5.32 us (1%)
    psum x1, waiting for transfers between devices, shards(): summed = lax.psum(packed_buffer, ALL)  129 us
    psum x1, waiting for transfers between devices, shards(): branch = lax.psum(out_buffer, ALL).reshape(steps, total, model_width)  126 us
    pmax x1, blocking collectives, shards(): peak = lax.pmax(peak_buffer, ALL)  41.3 us
    all_gather x1, blocking collectives, shards(): every = lax.all_gather(states, ALL, axis=0, tiled=False)  38.8 us
    all_gather x1, blocking collectives, shards(): query_all = lax.all_gather(own_query, 'seq', axis=2, tiled=True)  32.2 us
    psum x1, waiting for transfers between devices, shards(): lax.psum(jnp.concatenate([part_query, part_keyval, part_up], axis=1), 'req')  19.3 us
  transfers between devices with their start and end apart: 3, of which 3 were waited for; matrix products, arithmetic and copies ran while one was open for 1% of the time, Pallas kernels for 0%

commit v1 on v0

--- a/solution.py
+++ b/solution.py
@@ -6,6 +6,18 @@
 EPSILON = 1e-05
 NEGATIVE = -1e30
 ALL = ("req", "seq")
+
+
+def doubled_up(value, axis, dim):
+    ways, here = (lax.axis_size(axis), lax.axis_index(axis))
+    grown, reach = (value, 1)
+    while reach < ways:
+        theirs = lax.ppermute(grown, axis, [(d, d ^ reach) for d in range(ways)])
+        mine_first = jnp.concatenate([grown, theirs], axis=dim)
+        theirs_first = jnp.concatenate([theirs, grown], axis=dim)
+        grown = jnp.where(here & reach == 0, mine_first, theirs_first)
+        reach = 2 * reach
+    return grown
 
 
 def layer_norm(row_block, norm_gain, norm_bias):
@@ -77,7 +89,7 @@
     )
     up_part = first[:, slice_width + 2 * head_width :]
     own_query = lax.dynamic_slice_in_dim(query_raw, group_index * group_rows, group_rows, 1)
-    query_all = lax.all_gather(own_query, "seq", axis=2, tiled=True)
+    query_all = doubled_up(own_query, "seq", 2)
     flat_positions = positions.reshape(-1)
     query_rows = rotate(
         query_all.astype(jnp.float32).reshape(steps * group_rows, head_count, head_width),

time: 438 us -> 412 us (0.941)
  blocking collectives: 112 us -> 78.7 us
  waiting for transfers between devices: 274 us -> 282 us
  local copies, waits for them, and re-layouts: 22.3 us -> 16.9 us
  starting transfers between devices: 0.12 us -> 4.81 us
    all_gather x1 -> x0, blocking collectives: 32.2 us -> none  [shards(): query_all = lax.all_gather(own_query, 'seq', axis=2, tiled=True)]
    ppermute x0 -> x4, waiting for transfers between devices: none -> 8.58 us  [doubled_up(): theirs = lax.ppermute(grown, axis, [(d, d ^ reach) for d in range(ways)])]
    all_gather x1 -> x0, local copies, waits for them, and re-layouts: 5.18 us -> none  [shards(): query_all = lax.all_gather(own_query, 'seq', axis=2, tiled=True)]
    ppermute x0 -> x4, starting transfers between devices: none -> 4.69 us  [doubled_up(): theirs = lax.ppermute(grown, axis, [(d, d ^ reach) for d in range(ways)])]
  transfers between devices with their start and end apart: 3 -> 7, of which waited for: 3 -> 7; matrix products, arithmetic and copies ran while one was open for 1% -> 1% of each run, Pallas kernels for 0% -> 0%
where the time goes in v1:
time: 412 us; the launch traced here: 411 us
  waiting for transfers between devices  282 us (68%)
  blocking collectives  78.7 us (19%)
  local copies, waits for them, and re-layouts  16.9 us (4%)
  between operations  14.2 us (3%)
  matrix products  8.89 us (2%)
  other arithmetic  5.77 us (1%)
  starting transfers between devices  4.81 us (1%)
    psum x1, waiting for transfers between devices, shards(): summed = lax.psum(packed_buffer, ALL)  129 us
    psum x1, waiting for transfers between devices, shards(): branch = lax.psum(out_buffer, ALL).reshape(steps, total, model_width)  126 us
    pmax x1, blocking collectives, shards(): peak = lax.pmax(peak_buffer, ALL)  39.9 us
    all_gather x1, blocking collectives, shards(): every = lax.all_gather(states, ALL, axis=0, tiled=False)  38.8 us
    psum x1, waiting for transfers between devices, shards(): lax.psum(jnp.concatenate([part_query, part_keyval, part_up], axis=1), 'req')  19.2 us
    ppermute x4, waiting for transfers between devices, doubled_up(): theirs = lax.ppermute(grown, axis, [(d, d ^ reach) for d in range(ways)])  8.58 us
  transfers between devices with their start and end apart: 7, of which 7 were waited for; matrix products, arithmetic and copies ran while one was open for 1% of the time, Pallas kernels for 0%

profile of v1, /device:TPU:8, one launch (start us, length us, event | category | flops | bytes accessed | tf_op | source)
XLA Modules:
  0.0 411.4 jit_solution(739350821182533799)
XLA Ops:
  7.2 0.8 compare_select_fusion.2
  8.0 0.7 compare_and_fusion
  8.6 0.8 dynamic-slice.1
  9.4 0.8 dynamic-slice.2
  10.2 38.8 %all-gather = bf16[128,2,284]{2,1,0:T(2,128)(2,1)S(1)} all-gather(bf16[4,2,284]{2,1,0:T(2,128)(2,1)} %param.11), channel_id=2, replica_groups=mesh['req'=2,'seq'=16] {'req','seq'}, dimensions={0}, use_global_device_ids=true | all-gather | bytes 149952 | tf_op jit(solution)/shard_map/all_gather | solution.py:76
  49.0 0.3 reshape.355
  49.4 0.7 gather_fusion.1
  50.1 0.3 convert_reduce_fusion
  50.3 0.1 copy.67
  50.4 0.3 fusion.5
  50.7 0.1 copy.68
  51.1 0.1 broadcast_in_dim.144
  51.3 3.5 fusion.97
  54.8 0.3 fusion.95
  55.1 0.4 fusion.96
  55.5 0.8 concatenate.64
  56.5 0.6 gather_fusion
  57.4 0.1 multiply_cosine_fusion.1
  57.5 0.1 multiply_sine_fusion
  57.7 0.1 copy.74
  58.0 0.2 reshape.353
  58.4 19.2 %all-reduce.4.cloned.1.call-done = f32[16,1548]{1,0:T(8,128)} async-done(((f32[16,1548]{1,0:T(8,128)}), f32[16,1548]{1,0:T(8,128)}) %all-reduce.4.cloned.1.call-update) | async-done | bytes 99088 | tf_op jit(solution)/shard_map/psum | solution.py:85
  77.6 0.8 slice.99
  78.5 0.7 slice.124
  79.5 1.0 collective-permute-done
  80.5 0.1 broadcast_select_fusion.5
  80.6 1.5 collective-permute-start.1
  82.2 2.1 collective-permute-done.1
  84.3 0.1 broadcast_select_fusion.4
  84.4 0.6 collective-permute-start.2
  85.0 3.2 collective-permute-done.2
  88.2 0.1 broadcast_select_fusion.3
  88.4 2.5 collective-permute-start.3
  90.8 0.2 select_select_fusion
  91.0 2.2 collective-permute-done.3
  93.3 0.2 fusion.14
  93.4 0.2 reshape.362
  93.7 0.2 reshape.361
  93.9 0.1 fusion.99
  94.0 0.1 copy.81
  94.2 0.2 copy.71
  94.4 0.2 fusion.8
  94.5 0.2 copy.73
  94.7 0.1 reshape.357
  94.8 0.5 select_reduce_fusion
  95.4 39.9 %pmax.7 = f32[4,284]{1,0:T(4,128)S(1)} all-reduce(f32[4,284]{1,0:T(4,128)S(1)} %constant_dynamic-update-slice_fusion.1), channel_id=1, replica_groups=mesh['req'=2,'seq'=16] {'req','seq'}, use_global_device_ids=true, to_apply=%region_5.6 | all-reduce | flops 1136 | bytes 9088 | tf_op jit(solution)/shard_map/pmax | solution.py:133
  135.3 0.4 fusion
  135.7 0.4 convolution_multiply_fusion.1
  136.2 0.2 copy.75
  136.4 0.8 copy-done.2
  137.3 0.6 scatter_custom_fusion
  137.9 128.6 %all-reduce.6.cloned.1.call-done = f32[4,284,65]{2,1,0:T(8,128)} async-done(((f32[4,284,65]{2,1,0:T(8,128)}), f32[4,284,65]{2,1,0:T(8,128)}) %all-reduce.6.cloned.1.call-update) | async-done | bytes 295376 | tf_op jit(solution)/shard_map/psum | solution.py:143
  266.5 1.5 slice_reduce_fusion
  268.0 1.3 fusion.1
  269.3 0.2 convert_element_type.82
  269.6 0.4 fusion.56
  270.0 0.2 copy-done.6
  270.2 3.4 convolution_add_fusion
  273.7 1.3 dynamic_update_slice.11
  275.1 0.8 copy.77
  276.0 0.8 copy.79
  276.9 125.7 %all-reduce.8.cloned.1.call-done = f32[4,4,4544]{2,0,1:T(4,128)} async-done(((f32[4,4,4544]{2,0,1:T(4,128)}), f32[4,4,4544]{2,0,1:T(4,128)}) %all-reduce.8.cloned.1.call-update) | async-done | bytes 290832 | tf_op jit(solution)/shard_map/psum | solution.py:160
  402.5 1.6 gather_fusion.2
  404.2 0.6 copy.78
  (73 shorter events, 2.3 us)
Async XLA Ops:
  7.2 262.5 %copy-start = (bf16[284,2272]{1,0:T(8,128)(2,1)S(1)}, bf16[284,2272]{1,0:T(8,128)(2,1)}, u32[]{:S(2)}) copy-start(bf16[284,2272]{1,0:T(8,128)(2,1)} %param.19) | copy-start | bytes 3871492
  7.2 70.4 %all-reduce.4.cloned.1.call-start = ((), (), s32[]{:S(2)}) async-start(), calls=%async_computation | async-start | bytes 212992 | tf_op jit(solution)/shard_map/psum | solution.py:85
  51.3 3.5 copy-start.4
  51.3 3.8 copy-start.3
  54.8 1.6 copy-start.8
  54.8 1.7 copy-start.1
  55.1 2.6 copy-start.5
  56.3 210.2 %all-reduce.6.cloned.1.call-start = ((), (), s32[]{:S(2)}) async-start(), calls=%async_computation.1 | async-start | bytes 1179648 | tf_op jit(solution)/shard_map/psum | solution.py:143
  79.2 1.2 collective-permute-start
  80.6 3.7 collective-permute-start.1
  84.4 3.8 collective-permute-start.2
  88.4 4.9 %collective-permute-start.3 = (bf16[4,2,2272]{2,1,0:T(2,128)(2,1)S(1)}, bf16[4,2,2272]{2,1,0:T(2,128)(2,1)S(1)}, u32[]{:S(2)}, u32[]{:S(2)}) collective-permute-start(bf16[4,2,2272]{2,1,0:T(2,128)(2,1)S(1)} %broadcast_select_fusion.3), channel_id=1, source_target_pairs={{0,8},{1,9},{2,10},{3,11},{4,12},{5,13},{6,14},{7,15},{8,0},{9,1},... | collective-permute-start | bytes 109064 | tf_op jit(solution)/shard_map/ppermute | solution.py:15
  136.4 0.8 copy-start.2
  137.3 265.3 %all-reduce.8.cloned.1.call-start = ((), (), s32[]{:S(2)}) async-start(), calls=%async_computation.2 | async-start | bytes 589824 | tf_op jit(solution)/shard_map/psum | solution.py:160
  269.3 0.9 copy-start.6
  275.0 129.2 %copy-start.7 = (bf16[4,2,284]{2,1,0:T(2,128)(2,1)S(1)}, bf16[4,2,284]{2,1,0:T(2,128)(2,1)}, u32[]{:S(2)}) copy-start(bf16[4,2,284]{2,1,0:T(2,128)(2,1)} %param.11) | copy-start | bytes 13636
Sparse Core Ops, SparseCore 0:
  56.4 21.1 all-reduce.3
  137.4 129.0 all-reduce.5
  276.1 126.4 all-reduce.7
